TPU v7x, 512 devices: a whole 4x8x8 slice. The times are simulated.
512 devices in a mesh: ctx: 128 (over y, z, core), tp: 4 (over x).
Axes of the slice: x: 4, y: 8, z: 8, core: 2. Of those that a mesh axis runs over, the one named last changes fastest.
Arguments:
- hidden_in: bfloat16 [16384, 1536], P('ctx', 'tp'), may hold values from -60 to 60
- queries: bfloat16 [16384, 2048], P('ctx', 'tp'), may hold values from -200 to 200
- rotated_key_value: bfloat16 [16384, 4, 128], P('ctx', 'tp'), may hold values from -5 to 5
- sink_logit_table: float32 [32], P('tp'), may hold values from -2 to 2
- out_proj: bfloat16 [2048, 1536], P('tp', 'ctx'), may hold values from -0.125 to 0.125
- norm_gain: float32 [1536], P('tp'), may hold values from 0.1 to 1.9
- expert_in: bfloat16 [128, 2, 1536, 1536], P('ctx', None, None, 'tp'), may hold values from -0.15625 to 0.15625
- expert_out: bfloat16 [128, 1536, 1536], P('ctx', 'tp'), may hold values from -0.15625 to 0.15625
- routes: int32 [16384, 4], P('ctx'), may hold values from 0 to 127, all different within a row; in each aligned block of 128 rows (0 to 127, 128 to 255, ...) at most 12 rows name the same one
- route_scores: float32 [16384, 4], P('ctx'), may hold values from 0.05 to 1
Outputs:
- layer_out: bfloat16 [16384, 1536], P('ctx', 'tp')
Inputs may be any that keep to these rules, and one draw needn't show every extreme that they name: `routes`: each token names 4 different experts. In every aligned block of 128 tokens (the tokens of one device) no expert is named by more than 12 tokens, a bound that some block reaches.
All inputs are finite; a program needn't handle non-finite values.
Results may differ from a plain program's by a relative error of at most 0.008.
Values may be sent and summed in bfloat16 or wider, within the bound.
No kernel may reach another device: no remote copies, remote signals or barrier semaphores. Data moves between devices by JAX's collectives and lax.ppermute only.
A program may use at most 64 MiB of HBM per device.

v0:
```python
import jax
import jax.numpy as jnp
from jax import lax
from jax.sharding import PartitionSpec as P

WINDOW_KEYS = 128


def shifted(value, axis, steps):
    count = lax.axis_size(axis)
    first, last = (max(0, -steps), min(count, count - steps))
    return lax.ppermute(value, axis, [(source, source + steps) for source in range(first, last)])


def attend(query_block, key_blk, value_blk, inside, sink_row_block, factor):
    score = (
        jnp.einsum("rgqd,sgd->gqrs", query_block, key_blk, preferred_element_type=jnp.float32)
        * factor
    )
    masked = jnp.where(inside, score, -1e30)
    top_score = jnp.maximum(jnp.max(masked, -1), sink_row_block[:, :, None])
    expvals = jnp.where(inside, jnp.exp(score - top_score[..., None]), 0.0)
    denominator = jnp.sum(expvals, -1) + jnp.exp(sink_row_block[:, :, None] - top_score)
    probs = (expvals / denominator[..., None]).astype(jnp.bfloat16)
    mixed = jnp.einsum("gqrs,sgd->rgqd", probs, value_blk, preferred_element_type=jnp.float32)
    return mixed.astype(jnp.bfloat16)


def body(
    hidden_in,
    queries,
    rotated_key_value,
    sink_logit_table,
    out_proj,
    norm_gain,
    expert_in,
    expert_out,
    routes,
    route_scores,
):
    tok_rows = hidden_in.shape[0]
    kv_heads = rotated_key_value.shape[1]
    head_dim = rotated_key_value.shape[2] // 2
    q_heads = sink_logit_table.shape[0]
    queries_per_group = q_heads // kv_heads
    factor = head_dim ** (-0.5)
    sink_row_block = sink_logit_table.reshape(kv_heads, queries_per_group)
    earlier = shifted(rotated_key_value, "ctx", 1)
    keys_all = jnp.concatenate([earlier, rotated_key_value], 0)
    first_pos = lax.axis_index("ctx") * tok_rows
    block_row_count = min(512, tok_rows)
    query_block = queries.reshape(block_row_count, kv_heads, queries_per_group, head_dim)
    query_pos = first_pos + 0 + jnp.arange(block_row_count, dtype=jnp.int32)[:, None]
    key_pos = (
        first_pos
        + 0
        - WINDOW_KEYS
        + jnp.arange(block_row_count + WINDOW_KEYS, dtype=jnp.int32)[None, :]
    )
    inside = (key_pos <= query_pos) & (key_pos > query_pos - WINDOW_KEYS) & (key_pos >= 0)
    mixed = attend(
        query_block,
        keys_all[..., :head_dim],
        keys_all[..., head_dim:],
        inside,
        sink_row_block,
        factor,
    )
    outputs = mixed.reshape(block_row_count, q_heads * head_dim)
    head_partial = jnp.dot(
        outputs,
        lax.all_gather(out_proj, "ctx", axis=1, tiled=True),
        preferred_element_type=jnp.float32,
    )
    d_model = head_partial.shape[1]
    residual = hidden_in.astype(jnp.float32) + lax.psum_scatter(
        head_partial.astype(jnp.bfloat16), "tp", scatter_dimension=1, tiled=True
    ).astype(jnp.float32)
    square_total = lax.psum(jnp.sum(residual * residual, -1), "tp")
    normed = (residual * lax.rsqrt(square_total[:, None] / d_model + 1e-05) * norm_gain).astype(
        jnp.bfloat16
    )
    ctx_count = lax.axis_size("ctx")
    tp_count = lax.axis_size("tp")
    top_count = routes.shape[1]
    experts = ctx_count * expert_in.shape[0]
    capacity = max(2, min(tok_rows, 3 * top_count * tok_rows // experts))
    quarter_w = d_model // tp_count
    onehot = (routes[:, :, None] == jnp.arange(experts, dtype=jnp.int32)).astype(jnp.int32)
    per_tok = jnp.sum(onehot, 1)
    before = jnp.cumsum(per_tok, axis=0) - per_tok
    slot_ids = jnp.sum(onehot * before[:, None, :], -1)
    flat_index = (routes * capacity + slot_ids).reshape(-1)
    weights = route_scores / jnp.sum(route_scores, -1, keepdims=True)
    tp_index = lax.axis_index("tp")
    spread = jnp.broadcast_to(normed[:, None, :], (tok_rows, top_count, quarter_w)).reshape(
        -1, quarter_w
    )
    outbox = jnp.zeros((experts * capacity, quarter_w), jnp.bfloat16).at[flat_index].set(spread)
    arrived = lax.all_to_all(
        outbox.reshape(ctx_count, capacity, quarter_w), "ctx", 0, 0, tiled=True
    ).reshape(-1, quarter_w)
    pieces = [arrived]
    for step in range(1, tp_count):
        pieces.append(
            lax.ppermute(arrived, "tp", [(i, (i + step) % tp_count) for i in range(tp_count)])
        )
    row_data = jnp.concatenate(pieces, 1)
    order = (tp_index - jnp.arange(tp_count, dtype=jnp.int32)) % tp_count
    hidden_w = expert_in.shape[3]
    w_gate = jnp.take(
        expert_in[0, 0].reshape(tp_count, quarter_w, hidden_w), order, axis=0
    ).reshape(d_model, hidden_w)
    w_up = jnp.take(expert_in[0, 1].reshape(tp_count, quarter_w, hidden_w), order, axis=0).reshape(
        d_model, hidden_w
    )
    gate_vals = jnp.dot(row_data, w_gate, preferred_element_type=jnp.float32)
    up_vals = jnp.dot(row_data, w_up, preferred_element_type=jnp.float32)
    activated = ((up_vals + 1.0) * gate_vals * jax.nn.sigmoid(1.702 * gate_vals)).astype(
        jnp.bfloat16
    )

    def partial_for(quarter_id):
        cols = lax.dynamic_slice_in_dim(expert_out[0], quarter_id * quarter_w, quarter_w, 1)
        return jnp.dot(activated, cols, preferred_element_type=jnp.float32).astype(jnp.bfloat16)

    summed = partial_for(tp_index).astype(jnp.float32)
    for step in range(1, tp_count):
        piece = partial_for((tp_index + step) % tp_count)
        summed = summed + lax.ppermute(
            piece, "tp", [(i, (i + step) % tp_count) for i in range(tp_count)]
        ).astype(jnp.float32)
    result = summed.astype(jnp.bfloat16).reshape(ctx_count, capacity, quarter_w)
    returned = lax.all_to_all(result, "ctx", 0, 0, tiled=True).reshape(-1, quarter_w)
    expert_result = returned[flat_index].reshape(tok_rows, top_count, quarter_w)
    moe_sum = jnp.zeros((tok_rows, quarter_w), jnp.float32)
    for member in range(top_count):
        moe_sum = moe_sum + weights[:, member : member + 1] * expert_result[:, member].astype(
            jnp.float32
        )
    return (residual + moe_sum).astype(jnp.bfloat16)


def solution(mesh):
    in_specs = (
        P("ctx", "tp"),
        P("ctx", "tp"),
        P("ctx", "tp", None),
        P("tp"),
        P("tp", "ctx"),
        P("tp"),
        P("ctx", None, None, "tp"),
        P("ctx", "tp", None),
        P("ctx", None),
        P("ctx", None),
    )
    out_specs = P("ctx", "tp")
    return jax.shard_map(body, mesh=mesh, in_specs=in_specs, out_specs=out_specs, check_vma=False)
```

profile of v0, /device:TPU:8, one launch (start us, length us, event | category | flops | bytes accessed | tf_op | source)
XLA Modules:
  0.0 399.1 jit_solution(11350336013368773157)
XLA Ops:
  6.5 0.7 all-gather.3.cloned.1.call-update
  7.3 0.9 copy.35
  8.2 1.9 collective-permute-start
  10.1 0.1 and_and_fusion
  10.3 1.0 copy.37
  11.3 8.7 %collective-permute-done = bf16[128,1,128]{0,2,1:T(8,128)(2,1)S(1)} collective-permute-done((bf16[128,1,128]{0,2,1:T(8,128)(2,1)S(1)}, bf16[128,1,128]{0,2,1:T(8,128)(2,1)S(1)}, u32[]{:S(2)}, u32[]{:S(2)}) %collective-permute-start) | collective-permute-done | bytes 32800 | tf_op jit(solution)/shard_map/ppermute | solution.py:12
  20.0 0.3 select_reduce_fusion
  20.5 0.2 fusion.5
  20.7 0.1 exponential_add_fusion
  20.7 0.4 convolution_convert_fusion.5
  21.1 76.4 %all-gather.3.cloned.1.call-done = bf16[128,12,512]{2,1,0:T(8,128)(2,1)} async-done(((bf16[1,12,512]{2,1,0:T(8,128)(2,1)}), bf16[128,12,512]{2,1,0:T(8,128)(2,1)}) %all-gather.3.cloned.1.call-update) | async-done | bytes 1572880 | tf_op jit(solution)/shard_map/all_gather | solution.py:72
  97.5 2.5 reshape.245
  100.0 0.6 convolution_convert_fusion.4
  100.7 0.9 copy.44
  101.6 0.1 convert_reduce_fusion
  101.8 0.2 reduce_window_sum.11
  102.0 0.2 select_reduce_fusion.1
  102.2 0.1 copy.39
  102.3 0.1 reshape.197
  102.5 23.3 %reduce-scatter.4.cloned.1.call-done = bf16[384,128]{1,0:T(8,128)(2,1)} async-done(((bf16[1536,128]{1,0:T(8,128)(2,1)}), bf16[384,128]{1,0:T(8,128)(2,1)}) %reduce-scatter.4.cloned.1.call-update) | async-done | bytes 98320
  125.8 1.0 copy.45
  126.8 0.1 multiply_reduce_fusion
  126.9 8.4 %psum.7 = f32[128]{0:T(128)S(1)} all-reduce(f32[128]{0:T(128)S(1)} %multiply_reduce_fusion), channel_id=1, replica_groups=mesh['ctx'=128,'tp'=4] {'tp'}, use_global_device_ids=true, to_apply=%region_8.9 | all-reduce | flops 128 | bytes 1024 | tf_op jit(solution)/shard_map/psum | solution.py:79
  135.4 0.1 multiply_convert_fusion
  135.5 0.1 broadcast_in_dim.46
  135.6 0.1 reshape.238
  135.7 3.5 scatter_custom_fusion
  139.2 2.2 reshape.199
  141.4 56.4 %all_to_all.10 = bf16[128,12,384]{2,1,0:T(8,128)(2,1)} all-to-all(bf16[128,12,384]{2,1,0:T(8,128)(2,1)S(1)} %reshape.199), channel_id=1, replica_groups=mesh['ctx'=128,'tp'=4] {'ctx'}, dimensions={0} | all-to-all | bytes 2359296 | tf_op jit(solution)/shard_map/all_to_all | solution.py:100
  197.8 3.2 reshape.200
  201.0 3.2 collective-permute-start.1
  204.2 2.9 fusion.38
  207.2 3.4 collective-permute-start.2
  210.6 3.3 collective-permute-start.3
  213.9 0.8 gather_fusion.1
  214.8 2.1 gather_fusion.2
  216.9 0.3 broadcast_select_fusion.1
  217.2 1.4 constant_dynamic-update-slice_fusion.3
  218.6 36.9 %collective-permute-done.1 = bf16[1536,384]{1,0:T(8,128)(2,1)} collective-permute-done((bf16[1536,384]{1,0:T(8,128)(2,1)}, bf16[1536,384]{1,0:T(8,128)(2,1)}, u32[]{:S(2)}, u32[]{:S(2)}) %collective-permute-start.1) | collective-permute-done | bytes 1179680 | tf_op jit(solution)/shard_map/ppermute | solution.py:106
  255.5 1.5 constant_dynamic-update-slice_fusion.2
  257.0 1.5 constant_dynamic-update-slice_fusion.1
  258.6 2.4 collective-permute-done.3
  261.0 1.5 constant_dynamic-update-slice_fusion
  262.5 2.6 fusion.40
  265.1 3.1 fusion.2
  268.2 1.9 convolution_convert_fusion.2
  270.1 2.9 collective-permute-start.4
  273.0 1.9 convolution_convert_fusion.1
  274.9 5.0 %collective-permute-start.5 = (bf16[1536,384]{1,0:T(8,128)(2,1)}, bf16[1536,384]{1,0:T(8,128)(2,1)}, u32[]{:S(2)}, u32[]{:S(2)}) collective-permute-start(bf16[1536,384]{1,0:T(8,128)(2,1)} %convolution_convert_fusion.1), channel_id=1, source_target_pairs={{0,2},{1,3},{2,0},{3,1},{4,6},{5,7},{6,4},{7,5},{8,10},{9,11},{10,... | collective-permute-start | bytes 3538952 | tf_op jit(solution)/shard_map/ppermute | solution.py:130
  279.9 1.9 convolution_convert_fusion
  281.8 2.1 collective-permute-start.6
  283.9 17.1 %collective-permute-done.4 = bf16[1536,384]{1,0:T(8,128)(2,1)S(1)} collective-permute-done((bf16[1536,384]{1,0:T(8,128)(2,1)}, bf16[1536,384]{1,0:T(8,128)(2,1)S(1)}, u32[]{:S(2)}, u32[]{:S(2)}) %collective-permute-start.4) | collective-permute-done | bytes 1179680 | tf_op jit(solution)/shard_map/ppermute | solution.py:130
  301.0 26.6 %collective-permute-done.5 = bf16[1536,384]{1,0:T(8,128)(2,1)} collective-permute-done((bf16[1536,384]{1,0:T(8,128)(2,1)}, bf16[1536,384]{1,0:T(8,128)(2,1)}, u32[]{:S(2)}, u32[]{:S(2)}) %collective-permute-start.5) | collective-permute-done | bytes 1179680 | tf_op jit(solution)/shard_map/ppermute | solution.py:130
  327.6 3.3 collective-permute-done.6
  330.8 3.1 add_convert_fusion
  333.9 1.3 reshape.203
  335.2 9.0 %all-to-all-start.1 = ((bf16[128,12,384]{2,1,0:T(8,128)(2,1)}), bf16[128,12,384]{2,1,0:T(8,128)(2,1)}, u32[]{:S(2)}, u32[]{:S(2)}) async-start(bf16[128,12,384]{2,1,0:T(8,128)(2,1)} %reshape.203), calls=%async_computation.1 | async-start | bytes 3145728 | tf_op jit(solution)/shard_map/all_to_all | solution.py:134
  344.3 42.0 %all-to-all-done.1 = bf16[128,12,384]{2,1,0:T(8,128)(2,1)} async-done(((bf16[128,12,384]{2,1,0:T(8,128)(2,1)}), bf16[128,12,384]{2,1,0:T(8,128)(2,1)}, u32[]{:S(2)}, u32[]{:S(2)}) %all-to-all-start.1) | async-done | bytes 1179680 | tf_op jit(solution)/shard_map/all_to_all | solution.py:134
  386.3 2.3 reshape.204
  388.6 1.9 gather_fusion
  390.5 0.1 reshape.205
  390.6 0.6 fusion.39
  391.2 0.2 copy-done.2
  391.5 0.8 fusion.21
  (38 shorter events, 0.3 us)
Async XLA Ops:
  6.5 261.6 %copy-start = (bf16[1,384,1536]{2,1,0:T(8,128)(2,1)S(1)}, bf16[1,384,1536]{2,1,0:T(8,128)(2,1)}, u32[]{:S(2)}) copy-start(bf16[1,384,1536]{2,1,0:T(8,128)(2,1)} %param.19) | copy-start | bytes 3538948
  6.5 13.8 %copy-start.9 = (f32[8]{0:T(128)S(1)}, f32[8]{0:T(128)}, u32[]{:S(2)}) copy-start(f32[8]{0:T(128)} %param.15) | copy-start | bytes 100
  6.5 91.0 %all-gather.3.cloned.1.call-start = ((), (), s32[]{:S(2)}) async-start(), calls=%async_computation.3 | async-start | bytes 2113536 | tf_op jit(solution)/shard_map/all_gather | solution.py:72
  7.3 118.5 %reduce-scatter.4.cloned.1.call-start = ((), (), s32[]{:S(2)}) async-start(), calls=%async_computation.4 | async-start | bytes 491520
  8.2 11.9 %collective-permute-start = (bf16[128,1,128]{0,2,1:T(8,128)(2,1)S(1)}, bf16[128,1,128]{0,2,1:T(8,128)(2,1)S(1)}, u32[]{:S(2)}, u32[]{:S(2)}) collective-permute-start(bf16[128,1,128]{0,2,1:T(8,128)(2,1)S(1)} %copy.35), channel_id=1, source_target_pairs={{0,4},{4,8},{8,12},{12,16},{16,20},{20,24},{24,28},{28,32},{32,36}... | collective-permute-start | bytes 98312 | tf_op jit(solution)/shard_map/ppermute | solution.py:12
  100.0 1.6 copy-start.6
  100.6 26.2 %copy-start.4 = (bf16[128,384]{1,0:T(8,128)(2,1)S(1)}, bf16[128,384]{1,0:T(8,128)(2,1)}, u32[]{:S(2)}) copy-start(bf16[128,384]{1,0:T(8,128)(2,1)} %param.12) | copy-start | bytes 294916
  100.7 34.7 %copy-start.8 = (f32[384]{0:T(512)S(1)}, f32[384]{0:T(512)}, u32[]{:S(2)}) copy-start(f32[384]{0:T(512)} %param.17) | copy-start | bytes 4612
  126.8 8.9 %copy-start.1 = (bf16[128,384]{1,0:T(8,128)(2,1)}, bf16[128,384]{1,0:T(8,128)(2,1)S(1)}, u32[]{:S(2)}) copy-start(bf16[128,384]{1,0:T(8,128)(2,1)S(1)} %copy.45) | copy-start | bytes 294916
  201.0 54.5 %collective-permute-start.1 = (bf16[1536,384]{1,0:T(8,128)(2,1)}, bf16[1536,384]{1,0:T(8,128)(2,1)}, u32[]{:S(2)}, u32[]{:S(2)}) collective-permute-start(bf16[1536,384]{1,0:T(8,128)(2,1)} %reshape.200), channel_id=1, source_target_pairs={{0,1},{1,2},{2,3},{3,0},{4,5},{5,6},{6,7},{7,4},{8,9},{9,10},{10,1... | collective-permute-start | bytes 3538952 | tf_op jit(solution)/shard_map/ppermute | solution.py:106
  207.2 49.9 %collective-permute-start.2 = (bf16[1536,384]{1,0:T(8,128)(2,1)}, bf16[1536,384]{1,0:T(8,128)(2,1)}, u32[]{:S(2)}, u32[]{:S(2)}) collective-permute-start(bf16[1536,384]{1,0:T(8,128)(2,1)} %reshape.200), channel_id=1, source_target_pairs={{0,2},{1,3},{2,0},{3,1},{4,6},{5,7},{6,4},{7,5},{8,10},{9,11},{10,... | collective-permute-start | bytes 3538952 | tf_op jit(solution)/shard_map/ppermute | solution.py:106
  210.6 50.4 %collective-permute-start.3 = (bf16[1536,384]{1,0:T(8,128)(2,1)}, bf16[1536,384]{1,0:T(8,128)(2,1)}, u32[]{:S(2)}, u32[]{:S(2)}) collective-permute-start(bf16[1536,384]{1,0:T(8,128)(2,1)} %reshape.200), channel_id=1, source_target_pairs={{0,3},{1,0},{2,1},{3,2},{4,7},{5,4},{6,5},{7,6},{8,11},{9,8},{10,9... | collective-permute-start | bytes 3538952 | tf_op jit(solution)/shard_map/ppermute | solution.py:106
  270.1 30.9 %collective-permute-start.4 = (bf16[1536,384]{1,0:T(8,128)(2,1)}, bf16[1536,384]{1,0:T(8,128)(2,1)S(1)}, u32[]{:S(2)}, u32[]{:S(2)}) collective-permute-start(bf16[1536,384]{1,0:T(8,128)(2,1)} %convolution_convert_fusion.2), channel_id=1, source_target_pairs={{0,1},{1,2},{2,3},{3,0},{4,5},{5,6},{6,7},{7,4},{8,9},{9,10},{10,1... | collective-permute-start | bytes 3538952 | tf_op jit(solution)/shard_map/ppermute | solution.py:130
  274.9 52.6 %collective-permute-start.5 = (bf16[1536,384]{1,0:T(8,128)(2,1)}, bf16[1536,384]{1,0:T(8,128)(2,1)}, u32[]{:S(2)}, u32[]{:S(2)}) collective-permute-start(bf16[1536,384]{1,0:T(8,128)(2,1)} %convolution_convert_fusion.1), channel_id=1, source_target_pairs={{0,2},{1,3},{2,0},{3,1},{4,6},{5,7},{6,4},{7,5},{8,10},{9,11},{10,... | collective-permute-start | bytes 3538952 | tf_op jit(solution)/shard_map/ppermute | solution.py:130
  281.8 49.0 %collective-permute-start.6 = (bf16[1536,384]{1,0:T(8,128)(2,1)}, bf16[1536,384]{1,0:T(8,128)(2,1)}, u32[]{:S(2)}, u32[]{:S(2)}) collective-permute-start(bf16[1536,384]{1,0:T(8,128)(2,1)} %convolution_convert_fusion), channel_id=1, source_target_pairs={{0,3},{1,0},{2,1},{3,2},{4,7},{5,4},{6,5},{7,6},{8,11},{9,8},{10,9... | collective-permute-start | bytes 3538952 | tf_op jit(solution)/shard_map/ppermute | solution.py:130
  301.0 26.6 %copy-start.3 = (bf16[1536,384]{1,0:T(8,128)(2,1)}, bf16[1536,384]{1,0:T(8,128)(2,1)S(1)}, u32[]{:S(2)}) copy-start(bf16[1536,384]{1,0:T(8,128)(2,1)S(1)} %collective-permute-done.4) | copy-start | bytes 3538948
  335.2 9.1 %copy-start.7 = (f32[128,4]{0,1:T(4,128)S(1)}, f32[128,4]{0,1:T(4,128)}, u32[]{:S(2)}) copy-start(f32[128,4]{0,1:T(4,128)} %param.21) | copy-start | bytes 6148
  335.2 51.1 %all-to-all-start.1 = ((bf16[128,12,384]{2,1,0:T(8,128)(2,1)}), bf16[128,12,384]{2,1,0:T(8,128)(2,1)}, u32[]{:S(2)}, u32[]{:S(2)}) async-start(bf16[128,12,384]{2,1,0:T(8,128)(2,1)} %reshape.203), calls=%async_computation.1 | async-start | bytes 3145728 | tf_op jit(solution)/shard_map/all_to_all | solution.py:134
  390.5 0.9 copy-start.2
  390.5 0.9 copy-start.5
Sparse Core Ops, SparseCore 0:
  10.5 86.9 all-gather.2
  101.7 23.9 reduce-scatter.3
where the time goes:
time: 400 us; the launch traced here: 399 us
  waiting for transfers between devices  237 us (59%)
  blocking collectives  64.8 us (16%)
  local copies, waits for them, and re-layouts  33.3 us (8%)
  starting transfers between devices  30.9 us (8%)
  matrix products  15.8 us (4%)
  between operations  13.9 us (3%)
    all_gather x1, waiting for transfers between devices, body(): lax.all_gather(out_proj, 'ctx', axis=1, tiled=True)  76.4 us
    all_to_all x1, blocking collectives, body(): lax.all_to_all(outbox.reshape(ctx_count, capacity, quarter_w), 'ctx', 0,...  56.4 us
    ppermute x3, waiting for transfers between devices, body(): lax.ppermute(piece, 'tp', [(i, (i + step) % tp_count) for i in range(tp_c...  46.9 us
    all_to_all x1, waiting for transfers between devices, body(): lax.all_to_all(result, 'ctx', 0, 0, tiled=True).reshape(-1, quarter_w)  42 us
    ppermute x3, waiting for transfers between devices, body(): lax.ppermute(arrived, 'tp', [(i, (i + step) % tp_count) for i in range(tp...  39.3 us
    unnamed x3, waiting for transfers between devices  24.1 us
    unnamed x28, local copies, waits for them, and re-layouts  11 us
    ppermute x3, starting transfers between devices, body(): lax.ppermute(piece, 'tp', [(i, (i + step) % tp_count) for i in range(tp_c...  9.97 us
  transfers between devices with their start and end apart: 10, of which 9 were waited for; matrix products, arithmetic and copies ran while one was open for 5% of the time, Pallas kernels for 0%

commit v1 on v0

--- a/solution.py
+++ b/solution.py
@@ -69,7 +69,9 @@
     outputs = mixed.reshape(block_row_count, q_heads * head_dim)
     head_partial = jnp.dot(
         outputs,
-        lax.all_gather(out_proj, "ctx", axis=1, tiled=True),
+        jnp.concatenate(
+            lax.all_to_all(jnp.stack([out_proj] * lax.axis_size("ctx")), "ctx", 0, 0), axis=1
+        ),
         preferred_element_type=jnp.float32,
     )
     d_model = head_partial.shape[1]

time: 400 us -> 380 us (0.950)
  waiting for transfers between devices: 237 us -> 197 us
  starting transfers between devices: 30.9 us -> 48.4 us
    all_gather x1 -> x0, waiting for transfers between devices: 76.4 us -> none  [body(): lax.all_gather(out_proj, 'ctx', axis=1, tiled=True)]
    ppermute x1, waiting for transfers between devices: 8.72 us -> 42.7 us  [shifted(): lax.ppermute(value, axis, [(source, source + steps) for source in range(f...]
    all_to_all x0 -> x1, starting transfers between devices: none -> 17.5 us  [body(): lax.all_to_all(jnp.stack([out_proj] * lax.axis_size('ctx')), 'ctx', 0, 0)]
    all_to_all x0 -> x1, waiting for transfers between devices: none -> 5.22 us  [body(): lax.all_to_all(jnp.stack([out_proj] * lax.axis_size('ctx')), 'ctx', 0, 0)]
    unnamed x28 -> x29, local copies, waits for them, and re-layouts: 11 us -> 7.79 us
    unnamed x3 -> x2, waiting for transfers between devices: 24.1 us -> 21.3 us
where the time goes in v1:
time: 380 us; the launch traced here: 379 us
  waiting for transfers between devices  197 us (52%)
  blocking collectives  64.9 us (17%)
  starting transfers between devices  48.4 us (13%)
  local copies, waits for them, and re-layouts  33.8 us (9%)
  matrix products  17.3 us (5%)
  between operations  13.9 us (4%)
    all_to_all x1, blocking collectives, body(): lax.all_to_all(outbox.reshape(ctx_count, capacity, quarter_w), 'ctx', 0,...  56.4 us
    ppermute x3, waiting for transfers between devices, body(): lax.ppermute(piece, 'tp', [(i, (i + step) % tp_count) for i in range(tp_c...  46.9 us
    ppermute x1, waiting for transfers between devices, shifted(): lax.ppermute(value, axis, [(source, source + steps) for source in range(f...  42.7 us
    all_to_all x1, waiting for transfers between devices, body(): lax.all_to_all(result, 'ctx', 0, 0, tiled=True).reshape(-1, quarter_w)  42 us
    ppermute x3, waiting for transfers between devices, body(): lax.ppermute(arrived, 'tp', [(i, (i + step) % tp_count) for i in range(tp...  39.3 us
    unnamed x2, waiting for transfers between devices  21.3 us
    all_to_all x1, starting transfers between devices, body(): lax.all_to_all(jnp.stack([out_proj] * lax.axis_size('ctx')), 'ctx', 0, 0)  17.5 us
    ppermute x3, starting transfers between devices, body(): lax.ppermute(piece, 'tp', [(i, (i + step) % tp_count) for i in range(tp_c...  9.94 us
  transfers between devices with their start and end apart: 10, of which 9 were waited for; matrix products, arithmetic and copies ran while one was open for 5% of the time, Pallas kernels for 0%

profile of v1, /device:TPU:8, one launch (start us, length us, event | category | flops | bytes accessed | tf_op | source)
XLA Modules:
  0.0 378.7 jit_solution(17346620535380411034)
XLA Ops:
  6.5 2.4 stack.2
  9.0 17.5 %all-to-all-start = ((bf16[128,512,12]{1,2,0:T(8,128)(2,1)}), bf16[128,512,12]{1,2,0:T(8,128)(2,1)S(1)}, u32[]{:S(2)}, u32[]{:S(2)}) async-start(bf16[128,512,12]{1,2,0:T(8,128)(2,1)} %stack.2), calls=%async_computation | async-start | bytes 4194304 | tf_op jit(solution)/shard_map/all_to_all | solution.py:73
  26.5 0.1 copy.36
  26.6 2.0 collective-permute-start
  28.7 0.1 and_and_fusion
  28.9 1.0 copy.38
  29.9 42.7 %collective-permute-done = bf16[128,1,128]{0,2,1:T(8,128)(2,1)S(1)} collective-permute-done((bf16[128,1,128]{0,2,1:T(8,128)(2,1)S(1)}, bf16[128,1,128]{0,2,1:T(8,128)(2,1)S(1)}, u32[]{:S(2)}, u32[]{:S(2)}) %collective-permute-start) | collective-permute-done | bytes 32800 | tf_op jit(solution)/shard_map/ppermute | solution.py:12
  72.6 0.3 select_reduce_fusion
  73.0 0.2 fusion.5
  73.3 0.4 convolution_convert_fusion.5
  73.6 5.2 %all-to-all-done = bf16[128,512,12]{1,2,0:T(8,128)(2,1)S(1)} async-done(((bf16[128,512,12]{1,2,0:T(8,128)(2,1)}), bf16[128,512,12]{1,2,0:T(8,128)(2,1)S(1)}, u32[]{:S(2)}, u32[]{:S(2)}) %all-to-all-start) | async-done | bytes 1572896 | tf_op jit(solution)/shard_map/all_to_all | solution.py:73
  78.8 1.3 reshape.206
  80.2 2.1 convolution_convert_fusion.4
  82.3 0.9 copy.45
  83.3 0.1 convert_reduce_fusion
  83.4 0.2 reduce_window_sum.11
  83.6 0.2 select_reduce_fusion.1
  83.8 0.1 copy.40
  84.0 0.1 reshape.207
  84.1 21.3 %reduce-scatter.4.cloned.1.call-done = bf16[384,128]{1,0:T(8,128)(2,1)} async-done(((bf16[1536,128]{1,0:T(8,128)(2,1)}), bf16[384,128]{1,0:T(8,128)(2,1)}) %reduce-scatter.4.cloned.1.call-update) | async-done | bytes 98320
  105.3 1.0 copy.46
  106.4 0.1 multiply_reduce_fusion
  106.5 8.5 %psum.7 = f32[128]{0:T(128)S(1)} all-reduce(f32[128]{0:T(128)S(1)} %multiply_reduce_fusion), channel_id=1, replica_groups=mesh['ctx'=128,'tp'=4] {'tp'}, use_global_device_ids=true, to_apply=%region_8.9 | all-reduce | flops 128 | bytes 1024 | tf_op jit(solution)/shard_map/psum | solution.py:81
  115.0 0.1 multiply_convert_fusion
  115.1 0.1 broadcast_in_dim.46
  115.2 0.1 reshape.248
  115.3 3.5 scatter_custom_fusion
  118.8 2.2 reshape.209
  121.0 56.4 %all_to_all.15 = bf16[128,12,384]{2,1,0:T(8,128)(2,1)} all-to-all(bf16[128,12,384]{2,1,0:T(8,128)(2,1)S(1)} %reshape.209), channel_id=1, replica_groups=mesh['ctx'=128,'tp'=4] {'ctx'}, dimensions={0} | all-to-all | bytes 2359296 | tf_op jit(solution)/shard_map/all_to_all | solution.py:102
  177.4 3.2 reshape.210
  180.6 3.2 collective-permute-start.1
  183.8 2.9 fusion.38
  186.7 3.4 collective-permute-start.2
  190.1 3.3 collective-permute-start.3
  193.5 0.8 gather_fusion.1
  194.3 2.1 gather_fusion.2
  196.4 0.3 broadcast_select_fusion.1
  196.8 1.4 constant_dynamic-update-slice_fusion.3
  198.2 36.9 %collective-permute-done.1 = bf16[1536,384]{1,0:T(8,128)(2,1)} collective-permute-done((bf16[1536,384]{1,0:T(8,128)(2,1)}, bf16[1536,384]{1,0:T(8,128)(2,1)}, u32[]{:S(2)}, u32[]{:S(2)}) %collective-permute-start.1) | collective-permute-done | bytes 1179680 | tf_op jit(solution)/shard_map/ppermute | solution.py:108
  235.1 1.5 constant_dynamic-update-slice_fusion.2
  236.6 1.5 constant_dynamic-update-slice_fusion.1
  238.2 2.4 collective-permute-done.3
  240.6 1.5 constant_dynamic-update-slice_fusion
  242.1 2.6 fusion.40
  244.7 3.1 fusion.2
  247.8 1.9 convolution_convert_fusion.2
  249.7 2.9 collective-permute-start.4
  252.6 1.9 convolution_convert_fusion.1
  254.5 5.0 %collective-permute-start.5 = (bf16[1536,384]{1,0:T(8,128)(2,1)}, bf16[1536,384]{1,0:T(8,128)(2,1)}, u32[]{:S(2)}, u32[]{:S(2)}) collective-permute-start(bf16[1536,384]{1,0:T(8,128)(2,1)} %convolution_convert_fusion.1), channel_id=1, source_target_pairs={{0,2},{1,3},{2,0},{3,1},{4,6},{5,7},{6,4},{7,5},{8,10},{9,11},{10,... | collective-permute-start | bytes 3538952 | tf_op jit(solution)/shard_map/ppermute | solution.py:132
  259.5 1.9 convolution_convert_fusion
  261.4 2.1 collective-permute-start.6
  263.5 17.1 %collective-permute-done.4 = bf16[1536,384]{1,0:T(8,128)(2,1)S(1)} collective-permute-done((bf16[1536,384]{1,0:T(8,128)(2,1)}, bf16[1536,384]{1,0:T(8,128)(2,1)S(1)}, u32[]{:S(2)}, u32[]{:S(2)}) %collective-permute-start.4) | collective-permute-done | bytes 1179680 | tf_op jit(solution)/shard_map/ppermute | solution.py:132
  280.6 26.6 %collective-permute-done.5 = bf16[1536,384]{1,0:T(8,128)(2,1)} collective-permute-done((bf16[1536,384]{1,0:T(8,128)(2,1)}, bf16[1536,384]{1,0:T(8,128)(2,1)}, u32[]{:S(2)}, u32[]{:S(2)}) %collective-permute-start.5) | collective-permute-done | bytes 1179680 | tf_op jit(solution)/shard_map/ppermute | solution.py:132
  307.2 3.2 collective-permute-done.6
  310.4 3.1 add_convert_fusion
  313.5 1.3 reshape.213
  314.8 9.1 %all-to-all-start.2 = ((bf16[128,12,384]{2,1,0:T(8,128)(2,1)}), bf16[128,12,384]{2,1,0:T(8,128)(2,1)}, u32[]{:S(2)}, u32[]{:S(2)}) async-start(bf16[128,12,384]{2,1,0:T(8,128)(2,1)} %reshape.213), calls=%async_computation.2 | async-start | bytes 3145728 | tf_op jit(solution)/shard_map/all_to_all | solution.py:136
  323.9 42.0 %all-to-all-done.2 = bf16[128,12,384]{2,1,0:T(8,128)(2,1)} async-done(((bf16[128,12,384]{2,1,0:T(8,128)(2,1)}), bf16[128,12,384]{2,1,0:T(8,128)(2,1)}, u32[]{:S(2)}, u32[]{:S(2)}) %all-to-all-start.2) | async-done | bytes 1179680 | tf_op jit(solution)/shard_map/all_to_all | solution.py:136
  365.9 2.3 reshape.214
  368.2 1.9 gather_fusion
  370.1 0.1 reshape.215
  370.2 0.6 fusion.39
  370.8 0.2 copy-done.2
  371.1 0.8 fusion.21
  (40 shorter events, 0.4 us)
Async XLA Ops:
  6.5 241.2 %copy-start = (bf16[1,384,1536]{2,1,0:T(8,128)(2,1)S(1)}, bf16[1,384,1536]{2,1,0:T(8,128)(2,1)}, u32[]{:S(2)}) copy-start(bf16[1,384,1536]{2,1,0:T(8,128)(2,1)} %param.19) | copy-start | bytes 3538948
  8.9 17.6 %copy-start.6 = (bf16[128,1,128]{2,0,1:T(8,128)(2,1)S(1)}, bf16[128,1,128]{2,0,1:T(8,128)(2,1)}, u32[]{:S(2)}) copy-start(bf16[128,1,128]{2,0,1:T(8,128)(2,1)} %param.14) | copy-start | bytes 98308
  9.0 69.9 %all-to-all-start = ((bf16[128,512,12]{1,2,0:T(8,128)(2,1)}), bf16[128,512,12]{1,2,0:T(8,128)(2,1)S(1)}, u32[]{:S(2)}, u32[]{:S(2)}) async-start(bf16[128,512,12]{1,2,0:T(8,128)(2,1)} %stack.2), calls=%async_computation | async-start | bytes 4194304 | tf_op jit(solution)/shard_map/all_to_all | solution.py:73
  26.5 46.4 %copy-start.10 = (f32[8]{0:T(128)S(1)}, f32[8]{0:T(128)}, u32[]{:S(2)}) copy-start(f32[8]{0:T(128)} %param.15) | copy-start | bytes 100
  26.5 78.9 %reduce-scatter.4.cloned.1.call-start = ((), (), s32[]{:S(2)}) async-start(), calls=%async_computation.4 | async-start | bytes 491520
  26.6 45.9 %collective-permute-start = (bf16[128,1,128]{0,2,1:T(8,128)(2,1)S(1)}, bf16[128,1,128]{0,2,1:T(8,128)(2,1)S(1)}, u32[]{:S(2)}, u32[]{:S(2)}) collective-permute-start(bf16[128,1,128]{0,2,1:T(8,128)(2,1)S(1)} %copy.36), channel_id=1, source_target_pairs={{0,4},{4,8},{8,12},{12,16},{16,20},{20,24},{24,28},{28,32},{32,36}... | collective-permute-start | bytes 98312 | tf_op jit(solution)/shard_map/ppermute | solution.py:12
  80.2 3.1 copy-start.7
  82.3 24.1 %copy-start.4 = (bf16[128,384]{1,0:T(8,128)(2,1)S(1)}, bf16[128,384]{1,0:T(8,128)(2,1)}, u32[]{:S(2)}) copy-start(bf16[128,384]{1,0:T(8,128)(2,1)} %param.12) | copy-start | bytes 294916
  82.3 32.7 %copy-start.9 = (f32[384]{0:T(512)S(1)}, f32[384]{0:T(512)}, u32[]{:S(2)}) copy-start(f32[384]{0:T(512)} %param.17) | copy-start | bytes 4612
  106.4 8.9 %copy-start.1 = (bf16[128,384]{1,0:T(8,128)(2,1)}, bf16[128,384]{1,0:T(8,128)(2,1)S(1)}, u32[]{:S(2)}) copy-start(bf16[128,384]{1,0:T(8,128)(2,1)S(1)} %copy.46) | copy-start | bytes 294916
  180.6 54.5 %collective-permute-start.1 = (bf16[1536,384]{1,0:T(8,128)(2,1)}, bf16[1536,384]{1,0:T(8,128)(2,1)}, u32[]{:S(2)}, u32[]{:S(2)}) collective-permute-start(bf16[1536,384]{1,0:T(8,128)(2,1)} %reshape.210), channel_id=1, source_target_pairs={{0,1},{1,2},{2,3},{3,0},{4,5},{5,6},{6,7},{7,4},{8,9},{9,10},{10,1... | collective-permute-start | bytes 3538952 | tf_op jit(solution)/shard_map/ppermute | solution.py:108
  186.7 49.9 %collective-permute-start.2 = (bf16[1536,384]{1,0:T(8,128)(2,1)}, bf16[1536,384]{1,0:T(8,128)(2,1)}, u32[]{:S(2)}, u32[]{:S(2)}) collective-permute-start(bf16[1536,384]{1,0:T(8,128)(2,1)} %reshape.210), channel_id=1, source_target_pairs={{0,2},{1,3},{2,0},{3,1},{4,6},{5,7},{6,4},{7,5},{8,10},{9,11},{10,... | collective-permute-start | bytes 3538952 | tf_op jit(solution)/shard_map/ppermute | solution.py:108
  190.1 50.4 %collective-permute-start.3 = (bf16[1536,384]{1,0:T(8,128)(2,1)}, bf16[1536,384]{1,0:T(8,128)(2,1)}, u32[]{:S(2)}, u32[]{:S(2)}) collective-permute-start(bf16[1536,384]{1,0:T(8,128)(2,1)} %reshape.210), channel_id=1, source_target_pairs={{0,3},{1,0},{2,1},{3,2},{4,7},{5,4},{6,5},{7,6},{8,11},{9,8},{10,9... | collective-permute-start | bytes 3538952 | tf_op jit(solution)/shard_map/ppermute | solution.py:108
  249.7 30.9 %collective-permute-start.4 = (bf16[1536,384]{1,0:T(8,128)(2,1)}, bf16[1536,384]{1,0:T(8,128)(2,1)S(1)}, u32[]{:S(2)}, u32[]{:S(2)}) collective-permute-start(bf16[1536,384]{1,0:T(8,128)(2,1)} %convolution_convert_fusion.2), channel_id=1, source_target_pairs={{0,1},{1,2},{2,3},{3,0},{4,5},{5,6},{6,7},{7,4},{8,9},{9,10},{10,1... | collective-permute-start | bytes 3538952 | tf_op jit(solution)/shard_map/ppermute | solution.py:132
  254.5 52.6 %collective-permute-start.5 = (bf16[1536,384]{1,0:T(8,128)(2,1)}, bf16[1536,384]{1,0:T(8,128)(2,1)}, u32[]{:S(2)}, u32[]{:S(2)}) collective-permute-start(bf16[1536,384]{1,0:T(8,128)(2,1)} %convolution_convert_fusion.1), channel_id=1, source_target_pairs={{0,2},{1,3},{2,0},{3,1},{4,6},{5,7},{6,4},{7,5},{8,10},{9,11},{10,... | collective-permute-start | bytes 3538952 | tf_op jit(solution)/shard_map/ppermute | solution.py:132
  261.4 49.0 %collective-permute-start.6 = (bf16[1536,384]{1,0:T(8,128)(2,1)}, bf16[1536,384]{1,0:T(8,128)(2,1)}, u32[]{:S(2)}, u32[]{:S(2)}) collective-permute-start(bf16[1536,384]{1,0:T(8,128)(2,1)} %convolution_convert_fusion), channel_id=1, source_target_pairs={{0,3},{1,0},{2,1},{3,2},{4,7},{5,4},{6,5},{7,6},{8,11},{9,8},{10,9... | collective-permute-start | bytes 3538952 | tf_op jit(solution)/shard_map/ppermute | solution.py:132
  280.6 26.6 %copy-start.3 = (bf16[1536,384]{1,0:T(8,128)(2,1)}, bf16[1536,384]{1,0:T(8,128)(2,1)S(1)}, u32[]{:S(2)}) copy-start(bf16[1536,384]{1,0:T(8,128)(2,1)S(1)} %collective-permute-done.4) | copy-start | bytes 3538948
  314.8 9.1 %copy-start.8 = (f32[128,4]{0,1:T(4,128)S(1)}, f32[128,4]{0,1:T(4,128)}, u32[]{:S(2)}) copy-start(f32[128,4]{0,1:T(4,128)} %param.21) | copy-start | bytes 6148
  314.8 51.1 %all-to-all-start.2 = ((bf16[128,12,384]{2,1,0:T(8,128)(2,1)}), bf16[128,12,384]{2,1,0:T(8,128)(2,1)}, u32[]{:S(2)}, u32[]{:S(2)}) async-start(bf16[128,12,384]{2,1,0:T(8,128)(2,1)} %reshape.213), calls=%async_computation.2 | async-start | bytes 3145728 | tf_op jit(solution)/shard_map/all_to_all | solution.py:136
  370.1 0.9 copy-start.2
  370.1 0.9 copy-start.5
Sparse Core Ops, SparseCore 0:
  83.4 21.9 reduce-scatter.3
